TPU v7x, 256 devices: a whole 4x4x8 slice. The times are simulated.
256 devices in a mesh: pair: 16 (over z, core), virt: 16 (over x, y).
Axes of the slice: x: 4, y: 4, z: 8, core: 2. Of those that a mesh axis runs over, the one named last changes fastest.
Arguments:
- amplitudes: float32 [64, 2048, 4096], P('virt', 'pair'), may hold values from -0.9 to 0.9
- integrals: float32 [64, 384, 4096], P('virt', 'pair'), may hold values from -0.09375 to 0.09375
- tile_flags: int32 [64], P('virt'), may hold values 0 or 1
- live_count: int32 [16], replicated, may hold values from 1 to 4, as said below
- pair_occ: int32 [2048, 2], P(('pair', 'virt')), may hold values from 0 to 199
- occ_energy: float32 [200], replicated, may hold values from -2.5 to -0.3
- ab_energy: float32 [384], replicated, may hold values from 0.6 to 3
Outputs:
- ladder: float32 [2048, 384], P(('pair', 'virt'))
- update: float32 [2048, 384], P(('pair', 'virt'))
Inputs may be any that keep to these rules, and one draw needn't show every extreme that they name: `live_count`: entry v is how many of the 4 slots of virt index v hold tile pairs: its slots below that number do, and the contents of the others are not to be used. At some index it is 4, and at the index half the axis away it is 1.
All inputs are finite; a program needn't handle non-finite values. No bound on the sum of `tile_flags` on one device may be relied on, other than what follows from the above.
Results may differ from a plain program's by a relative error of at most 0.0001.
Values sent between devices are 32-bit elements; how exact they have to be, the bound alone decides.
No kernel may reach another device: no remote copies, remote signals or barrier semaphores. Data moves between devices by JAX's collectives and lax.ppermute only.
A program may use at most 128 MiB of HBM per device.

v0:
```python
import jax
import jax.numpy as jnp
from jax import lax
from jax.sharding import PartitionSpec as P

TILE = 64


def swap_in_tile(rows):
    shaped = rows.reshape(rows.shape[0], TILE, TILE)
    return jnp.swapaxes(shaped, 1, 2).reshape(rows.shape)


def symmetric_amps(amp_rows, flag):
    return amp_rows + flag.astype(jnp.float32) * swap_in_tile(amp_rows)


def tile_product(amp_tile, int_rows, precision=lax.Precision.HIGH):
    return lax.dot_general(
        amp_tile,
        int_rows,
        (((1,), (1,)), ((), ())),
        precision=precision,
        preferred_element_type=jnp.float32,
    )


def on_device(amplitudes, integrals, tile_flags, live_count, pair_occ, occ_energy, ab_energy):
    slots, pair_rows, _ = amplitudes.shape
    n_virt = lax.axis_size("virt")
    half = n_virt // 2
    virt_index = lax.axis_index("virt")
    partner = (virt_index + half) % n_virt
    columns = jnp.arange(n_virt, dtype=jnp.int32)
    neighbour = columns ^ 1
    across = jnp.roll(live_count, half)
    give_one = jnp.clip((live_count - across) // 2, 0, 1)
    take_one = jnp.clip((across - live_count) // 2, 0, 1)
    keep_one = live_count - give_one
    give_two = ((keep_one == 4) & (take_one[neighbour] == 0) & (keep_one[neighbour] <= 2)).astype(
        jnp.int32
    )
    take_two = give_two[neighbour]
    keep_all = keep_one - give_two
    own_count = live_count[virt_index]
    take = take_one[virt_index]
    take_y = take_two[virt_index]
    keep = keep_all[virt_index]
    send_at = own_count - 1
    send_amp = symmetric_amps(
        lax.dynamic_index_in_dim(amplitudes, send_at, 0, keepdims=False),
        lax.dynamic_index_in_dim(tile_flags, send_at, 0, keepdims=False),
    )
    send_int = lax.dynamic_index_in_dim(integrals, send_at, 0, keepdims=False)
    perm = [(v, (v + half) % n_virt) for v in range(n_virt)]
    recv_int = lax.ppermute(send_int, "virt", perm)
    recv_amp = lax.ppermute(send_amp, "virt", perm)
    perm_y = [(v, v ^ 1) for v in range(n_virt)]
    recv_int_y = lax.ppermute(integrals[3], "virt", perm_y)
    recv_amp_y = lax.ppermute(symmetric_amps(amplitudes[3], tile_flags[3]), "virt", perm_y)

    def own_amps(slot):
        return symmetric_amps(amplitudes[slot], tile_flags[slot])

    first_two = lax.all_gather(integrals[0:2], "pair", axis=1, tiled=True)
    running = tile_product(own_amps(0), first_two[0], lax.Precision.HIGHEST)
    second = tile_product(own_amps(1), first_two[1], lax.Precision.HIGHEST)
    running = running + jnp.where(keep > 1, second, jnp.zeros_like(second))
    third_int = jnp.where(take > 0, recv_int, jnp.where(take_y > 0, recv_int_y, integrals[2]))
    third_amp = jnp.where(take > 0, recv_amp, jnp.where(take_y > 0, recv_amp_y, own_amps(2)))
    third = tile_product(third_amp, lax.all_gather(third_int, "pair", axis=0, tiled=True))
    third_live = (take > 0) | (take_y > 0) | (keep > 2)
    running = running + jnp.where(third_live, third, jnp.zeros_like(third))

    def fourth(acc):
        gathered = lax.all_gather(integrals[3], "pair", axis=0, tiled=True)
        term = tile_product(own_amps(3), gathered)
        return acc + jnp.where(keep > 3, term, jnp.zeros_like(term))

    any_full = jnp.max(keep_all) > 3
    running = lax.cond(any_full, fourth, lambda acc: acc, running)
    ab = running.shape[1]
    blocks = running.reshape(n_virt, pair_rows // n_virt, ab)
    received = lax.all_to_all(blocks, "virt", 0, 0, tiled=False)
    ladder = jnp.sum(received, axis=0)
    occ_range = jnp.arange(occ_energy.shape[0], dtype=jnp.int32)
    first_energy = jnp.sum(
        jnp.where(pair_occ[:, 0:1] == occ_range[None, :], occ_energy[None, :], 0.0), axis=1
    )
    second_energy = jnp.sum(
        jnp.where(pair_occ[:, 1:2] == occ_range[None, :], occ_energy[None, :], 0.0), axis=1
    )
    denominator = ab_energy[None, :] - first_energy[:, None] - second_energy[:, None]
    return (ladder, ladder / denominator)


def solution(mesh):
    return jax.shard_map(
        on_device,
        mesh=mesh,
        in_specs=(
            P("virt", "pair", None),
            P("virt", "pair", None),
            P("virt"),
            P(),
            P(("pair", "virt"), None),
            P(),
            P(),
        ),
        out_specs=(P(("pair", "virt"), None), P(("pair", "virt"), None)),
        check_vma=False,
    )
```

profile of v0, /device:TPU:1, one launch (start us, length us, event | category | flops | bytes accessed | tf_op | source)
XLA Modules:
  0.0 164.5 jit_solution(631864503196057487)
XLA Ops:
  7.2 2.2 %slice.66 = f32[2,24,4096]{2,1,0:T(8,128)} slice(f32[4,24,4096]{2,1,0:T(8,128)} %param.10), slice={[0:2], [0:24], [0:4096]} | slice | bytes 1572864 | tf_op jit(solution)/shard_map/slice | solution.py:65
  11.5 3.6 %collective-permute-start.2 = (f32[24,4096]{1,0:T(8,128)S(1)}, f32[24,4096]{1,0:T(8,128)S(1)}, u32[]{:S(2)}, u32[]{:S(2)}) collective-permute-start(f32[24,4096]{1,0:T(8,128)S(1)} %get-tuple-element.42), channel_id=1, source_target_pairs={{0,8},{1,9},{2,10},{3,11},{4,12},{5,13},{6,14},{7,15},{8,0},{9,1},... | collective-permute-start | bytes 1179656 | tf_op jit(solution)/shard_map/ppermute | solution.py:56
  22.9 1.9 %collective-permute-done.3 = f32[24,4096]{1,0:T(8,128)S(1)} collective-permute-done((f32[24,4096]{1,0:T(8,128)S(1)}, f32[24,4096]{1,0:T(8,128)S(1)}, u32[]{:S(2)}, u32[]{:S(2)}) %collective-permute-start.3) | collective-permute-done | bytes 393248 | tf_op jit(solution)/shard_map/ppermute | solution.py:59
  25.7 8.3 %fusion.25 = (f32[1,128,4096]{2,1,0:T(8,128)}, f32[1,128,4096]{2,1,0:T(8,128)}, f32[1,128,4096]{2,1,0:T(8,128)}, f32[1,128,4096]{2,1,0:T(8,128)}, f32[1,128,4096]{2,1,0:T(8,128)}) fusion(f32[4,128,4096]{2,1,0:T(8,128)} %param.9, s32[]{:T(128)S(6)} %select_n.101), kind=kLoop, calls=%fused_computation.59 | loop fusion | bytes 20971524 | tf_op jit(solution)/shard_map/slice | solution.py:63
  34.0 1.9 %copy.41 = f32[1,128,4096]{1,2,0:T(8,128)S(1)} copy(f32[1,128,4096]{2,1,0:T(8,128)} %get-tuple-element.38) | data formatting | bytes 4194304
  40.3 2.1 %collective-permute-start = (f32[128,4096]{0,1:T(8,128)}, f32[128,4096]{0,1:T(8,128)}, u32[]{:S(2)}, u32[]{:S(2)}) collective-permute-start(f32[128,4096]{0,1:T(8,128)} %bitcast_add_fusion.3), channel_id=1, source_target_pairs={{0,8},{1,9},{2,10},{3,11},{4,12},{5,13},{6,14},{7,15},{8,0},{9,1},... | collective-permute-start | bytes 6291464 | tf_op jit(solution)/shard_map/ppermute | solution.py:57
  42.4 1.9 %copy.42 = f32[1,128,4096]{1,2,0:T(8,128)S(1)} copy(f32[1,128,4096]{2,1,0:T(8,128)} %get-tuple-element.37) | data formatting | bytes 4194304
  49.1 1.9 %copy.43 = f32[1,128,4096]{1,2,0:T(8,128)S(1)} copy(f32[1,128,4096]{2,1,0:T(8,128)} %get-tuple-element.36) | data formatting | bytes 4194304
  52.3 2.5 %copy.37 = f32[128,64,64]{0,2,1:T(8,128)} copy(f32[128,64,64]{0,1,2:T(8,128)S(1)} %bitcast.100) | data formatting | bytes 4194304 | tf_op jit(solution)/shard_map/mul | solution.py:15
  54.8 1.9 %copy.40 = f32[1,128,4096]{1,2,0:T(8,128)S(1)} copy(f32[1,128,4096]{2,1,0:T(8,128)} %get-tuple-element.39) | data formatting | bytes 4194304
  57.6 2.6 %copy.31 = f32[128,64,64]{0,2,1:T(8,128)} copy(f32[128,64,64]{0,1,2:T(8,128)S(1)} %bitcast.101) | data formatting | bytes 4194304 | tf_op jit(solution)/shard_map/mul | solution.py:15
  60.7 2.9 %copy.39 = f32[1,128,4096]{1,2,0:T(8,128)} copy(f32[1,128,4096]{2,1,0:T(8,128)} %get-tuple-element.40) | data formatting | bytes 4194304
  64.2 1.8 %broadcast_multiply_fusion.4 = f32[1,128,4096]{1,2,0:T(8,128)S(1)} fusion(f32[1,128,4096]{1,2,0:T(8,128)} %copy.39, f32[]{:T(128)} %bitcast.7), kind=kLoop, calls=%fused_computation.30 | loop fusion | flops 524288 | bytes 4194308 | tf_op jit(solution)/shard_map/mul | solution.py:15
  66.0 2.5 %copy.29 = f32[128,64,64]{0,2,1:T(8,128)} copy(f32[128,64,64]{0,1,2:T(8,128)S(1)} %bitcast.102) | data formatting | bytes 4194304 | tf_op jit(solution)/shard_map/mul | solution.py:15
  70.5 3.4 %bitcast_add_fusion.4 = f32[1,128,4096]{1,2,0:T(8,128)} fusion(f32[1,128,4096]{1,2,0:T(8,128)S(1)} %copy.40, f32[128,64,64]{0,2,1:T(8,128)} %copy.31), kind=kLoop, calls=%fused_computation.19 | loop fusion | flops 524288 | bytes 6291456 | tf_op jit(solution)/shard_map/add | solution.py:15
  75.5 11.9 %collective-permute-done = f32[128,4096]{0,1:T(8,128)} collective-permute-done((f32[128,4096]{0,1:T(8,128)}, f32[128,4096]{0,1:T(8,128)}, u32[]{:S(2)}, u32[]{:S(2)}) %collective-permute-start) | collective-permute-done | bytes 2097184 | tf_op jit(solution)/shard_map/ppermute | solution.py:57
  87.4 6.4 %collective-permute-done.1 = f32[128,4096]{0,1:T(8,128)} collective-permute-done((f32[128,4096]{0,1:T(8,128)}, f32[128,4096]{0,1:T(8,128)}, u32[]{:S(2)}, u32[]{:S(2)}) %collective-permute-start.1) | collective-permute-done | bytes 2097184 | tf_op jit(solution)/shard_map/ppermute | solution.py:60
  93.8 2.3 %fusion.11 = f32[128,4096]{0,1:T(8,128)} fusion(f32[128,4096]{0,1:T(8,128)} %collective-permute-done, f32[128,4096]{0,1:T(8,128)} %collective-permute-done.1, f32[128,64,64]{0,2,1:T(8,128)S(1)} %copy-done.7, f32[1,128,4096]{1,2,0:T(8,128)S(1)} %copy-done.2, pred[]{:T(512)} %bitcast.21, pred[]{:T(512)} %bitcast.20), kind=kLoop, calls=%fused_computation.15 | loop fusion | flops 1572864 | bytes 10485762 | tf_op jit(solution)/shard_map/jit(_where)/select_n | solution.py:70
  96.1 9.5 %fusion.17 = f32[128,384]{1,0:T(8,128)S(1)} fusion(f32[2,384,4096]{2,1,0:T(8,128)} %all-gather.7.cloned.1.call-done, f32[1,128,4096]{1,2,0:T(8,128)S(1)} %copy-done.4, pred[]{:T(512)S(6)} %gt.29), kind=kOutput, calls=%fused_computation.23 | convolution fusion | flops 2415968256 | bytes 8585217 | tf_op jit(solution)/shard_map/dot_general | solution.py:19
  105.7 9.8 %fusion.14 = f32[128,384]{1,0:T(8,128)S(1)} fusion(f32[128,384]{1,0:T(8,128)S(1)} %fusion.17, f32[2,384,4096]{2,1,0:T(8,128)} %all-gather.7.cloned.1.call-done, f32[1,128,4096]{1,2,0:T(8,128)S(1)} %copy-done.5), kind=kOutput, calls=%fused_computation.22 | convolution fusion | flops 2415968256 | bytes 8781824 | tf_op jit(solution)/shard_map/dot_general | solution.py:19
  115.5 20.6 %all-gather.9.cloned.1.call-done = f32[384,4096]{1,0:T(8,128)} async-done(((f32[24,4096]{1,0:T(8,128)}), f32[384,4096]{1,0:T(8,128)}) %all-gather.9.cloned.1.call-update) | async-done | bytes 6291472 | tf_op jit(solution)/shard_map/all_gather | solution.py:71
  136.1 7.1 %fusion.20 = f32[128,384]{1,0:T(8,128)} fusion(f32[128,384]{1,0:T(8,128)S(1)} %fusion.14, f32[128,4096]{0,1:T(8,128)S(1)} %copy-done.6, f32[384,4096]{1,0:T(8,128)} %all-gather.9.cloned.1.call-done, pred[]{:T(512)S(6)} %or.7), kind=kOutput, calls=%fused_computation.25 | convolution fusion | flops 1208057856 | bytes 8781825 | tf_op jit(solution)/shard_map/dot_general | solution.py:19
  143.2 6.7 %all-to-all-start = ((f32[16,8,384]{2,1,0:T(8,128)}), f32[16,8,384]{2,1,0:T(8,128)S(1)}, u32[]{:S(2)}, u32[]{:S(2)}) async-start(f32[16,8,384]{2,1,0:T(8,128)} %bitcast.42), calls=%async_computation | async-start | bytes 393216 | tf_op jit(solution)/shard_map/all_to_all | solution.py:84
  150.1 6.8 %all-to-all-done = f32[16,8,384]{2,1,0:T(8,128)S(1)} async-done(((f32[16,8,384]{2,1,0:T(8,128)}), f32[16,8,384]{2,1,0:T(8,128)S(1)}, u32[]{:S(2)}, u32[]{:S(2)}) %all-to-all-start) | async-done | bytes 196640 | tf_op jit(solution)/shard_map/all_to_all | solution.py:84
  (67 shorter events, 19.8 us)
Async XLA Ops:
  7.2 4.2 %copy-start.8 = (f32[4,24,4096]{2,1,0:T(8,128)S(1)}, f32[4,24,4096]{2,1,0:T(8,128)}, u32[]{:S(2)}) copy-start(f32[4,24,4096]{2,1,0:T(8,128)} %param.10) | copy-start | bytes 4718596
  7.2 2.3 %copy-start.11 = (s32[16]{0:T(128)S(1)}, s32[16]{0:T(128)}, u32[]{:S(2)}) copy-start(s32[16]{0:T(128)} %param.12) | copy-start | bytes 196
  7.2 88.9 %all-gather.7.cloned.1.call-start = ((), (), s32[]{:S(2)}) async-start(), calls=%async_computation.2 | async-start | bytes 13369344 | tf_op jit(solution)/shard_map/all_gather | solution.py:65
  9.4 126.7 %all-gather.9.cloned.1.call-start = ((), (), s32[]{:S(2)}) async-start(), calls=%async_computation.3 | async-start | bytes 6684672 | tf_op jit(solution)/shard_map/all_gather | solution.py:71
  11.5 11.4 %collective-permute-start.2 = (f32[24,4096]{1,0:T(8,128)S(1)}, f32[24,4096]{1,0:T(8,128)S(1)}, u32[]{:S(2)}, u32[]{:S(2)}) collective-permute-start(f32[24,4096]{1,0:T(8,128)S(1)} %get-tuple-element.42), channel_id=1, source_target_pairs={{0,8},{1,9},{2,10},{3,11},{4,12},{5,13},{6,14},{7,15},{8,0},{9,1},... | collective-permute-start | bytes 1179656 | tf_op jit(solution)/shard_map/ppermute | solution.py:56
  15.1 9.7 %collective-permute-start.3 = (f32[24,4096]{1,0:T(8,128)S(1)}, f32[24,4096]{1,0:T(8,128)S(1)}, u32[]{:S(2)}, u32[]{:S(2)}) collective-permute-start(f32[24,4096]{1,0:T(8,128)S(1)} %get-tuple-element.41), channel_id=1, source_target_pairs={{0,1},{1,0},{2,3},{3,2},{4,5},{5,4},{6,7},{7,6},{8,9},{9,8},{10,11... | collective-permute-start | bytes 1179656 | tf_op jit(solution)/shard_map/ppermute | solution.py:59
  34.0 1.9 %copy-start.10 = (s32[4]{0:T(128)S(1)}, s32[4]{0:T(128)}, u32[]{:S(2)}) copy-start(s32[4]{0:T(128)} %param.11) | copy-start | bytes 52
  40.3 47.1 %collective-permute-start = (f32[128,4096]{0,1:T(8,128)}, f32[128,4096]{0,1:T(8,128)}, u32[]{:S(2)}, u32[]{:S(2)}) collective-permute-start(f32[128,4096]{0,1:T(8,128)} %bitcast_add_fusion.3), channel_id=1, source_target_pairs={{0,8},{1,9},{2,10},{3,11},{4,12},{5,13},{6,14},{7,15},{8,0},{9,1},... | collective-permute-start | bytes 6291464 | tf_op jit(solution)/shard_map/ppermute | solution.py:57
  47.8 46.0 %collective-permute-start.1 = (f32[128,4096]{0,1:T(8,128)}, f32[128,4096]{0,1:T(8,128)}, u32[]{:S(2)}, u32[]{:S(2)}) collective-permute-start(f32[128,4096]{0,1:T(8,128)} %bitcast_add_fusion.2), channel_id=1, source_target_pairs={{0,1},{1,0},{2,3},{3,2},{4,5},{5,4},{6,7},{7,6},{8,9},{9,8},{10,11... | collective-permute-start | bytes 6291464 | tf_op jit(solution)/shard_map/ppermute | solution.py:60
  51.0 1.3 copy-start.1
  70.5 3.5 %copy-start = (f32[1,128,4096]{1,2,0:T(8,128)S(1)}, f32[1,128,4096]{1,2,0:T(8,128)}, u32[]{:S(2)}) copy-start(f32[1,128,4096]{1,2,0:T(8,128)} %copy.39) | copy-start | bytes 6291460
  70.5 3.5 %copy-start.3 = (f32[128,64,64]{0,2,1:T(8,128)S(1)}, f32[128,64,64]{0,2,1:T(8,128)}, u32[]{:S(2)}) copy-start(f32[128,64,64]{0,2,1:T(8,128)} %copy.29) | copy-start | bytes 6291460
  74.0 19.9 %copy-start.2 = (f32[1,128,4096]{1,2,0:T(8,128)S(1)}, f32[1,128,4096]{1,2,0:T(8,128)}, u32[]{:S(2)}) copy-start(f32[1,128,4096]{1,2,0:T(8,128)} %copy-done.1) | copy-start | bytes 6291460
  74.0 19.9 %copy-start.7 = (f32[128,64,64]{0,2,1:T(8,128)S(1)}, f32[128,64,64]{0,2,1:T(8,128)}, u32[]{:S(2)}) copy-start(f32[128,64,64]{0,2,1:T(8,128)} %copy.37) | copy-start | bytes 6291460
  75.5 20.6 %copy-start.4 = (f32[1,128,4096]{1,2,0:T(8,128)S(1)}, f32[1,128,4096]{1,2,0:T(8,128)}, u32[]{:S(2)}) copy-start(f32[1,128,4096]{1,2,0:T(8,128)} %bitcast_add_fusion.4) | copy-start | bytes 6291460
  96.1 9.5 %copy-start.5 = (f32[1,128,4096]{1,2,0:T(8,128)S(1)}, f32[1,128,4096]{1,2,0:T(8,128)}, u32[]{:S(2)}) copy-start(f32[1,128,4096]{1,2,0:T(8,128)} %bitcast_add_fusion.5) | copy-start | bytes 6291460
  105.7 30.4 %copy-start.6 = (f32[128,4096]{0,1:T(8,128)S(1)}, f32[128,4096]{0,1:T(8,128)}, u32[]{:S(2)}) copy-start(f32[128,4096]{0,1:T(8,128)} %fusion.11) | copy-start | bytes 6291460
  143.2 6.7 %copy-start.14 = (s32[8,2]{0,1:T(2,128)S(1)}, s32[8,2]{0,1:T(2,128)}, u32[]{:S(2)}) copy-start(s32[8,2]{0,1:T(2,128)} %param.13) | copy-start | bytes 196
  143.2 6.7 %copy-start.13 = (f32[200]{0:T(256)S(1)}, f32[200]{0:T(256)}, u32[]{:S(2)}) copy-start(f32[200]{0:T(256)} %param.14) | copy-start | bytes 2404
  143.2 13.7 %copy-start.12 = (f32[384]{0:T(512)S(1)}, f32[384]{0:T(512)}, u32[]{:S(2)}) copy-start(f32[384]{0:T(512)} %param.15) | copy-start | bytes 4612
  143.2 13.7 %all-to-all-start = ((f32[16,8,384]{2,1,0:T(8,128)}), f32[16,8,384]{2,1,0:T(8,128)S(1)}, u32[]{:S(2)}, u32[]{:S(2)}) async-start(f32[16,8,384]{2,1,0:T(8,128)} %bitcast.42), calls=%async_computation | async-start | bytes 393216 | tf_op jit(solution)/shard_map/all_to_all | solution.py:84
  156.9 0.7 copy-start.9
Sparse Core Ops, SparseCore 0:
  9.8 79.7 all-gather.6
  91.5 44.5 all-gather.8
where the time goes:
time: 165 us; the launch traced here: 164 us
  waiting for transfers between devices  48.7 us (30%)
  local copies, waits for them, and re-layouts  36.9 us (22%)
  matrix products  26.5 us (16%)
  between operations  22 us (13%)
  other arithmetic  15.4 us (9%)
  starting transfers between devices  15 us (9%)
    dot_general x3, matrix products, tile_product(): lax.dot_general(amp_tile, int_rows, (((1,), (1,)), ((), ())), precision=p...  26.5 us
    all_gather x1, waiting for transfers between devices, on_device(): lax.all_gather(third_int, 'pair', axis=0, tiled=True)  20.6 us
    ppermute x1, waiting for transfers between devices, on_device(): recv_amp = lax.ppermute(send_amp, 'virt', perm)  11.9 us
    unnamed x35, local copies, waits for them, and re-layouts  11.2 us
    mul x5, local copies, waits for them, and re-layouts, symmetric_amps(): return amp_rows + flag.astype(jnp.float32) * swap_in_tile(amp_rows)  10 us
    slice x2, local copies, waits for them, and re-layouts, own_amps(): return symmetric_amps(amplitudes[slot], tile_flags[slot])  8.97 us
    add x4, other arithmetic, symmetric_amps(): return amp_rows + flag.astype(jnp.float32) * swap_in_tile(amp_rows)  8.24 us
    all_to_all x1, waiting for transfers between devices, on_device(): received = lax.all_to_all(blocks, 'virt', 0, 0, tiled=False)  6.75 us
  transfers between devices with their start and end apart: 7, of which 6 were waited for; matrix products, arithmetic and copies ran while one was open for 41% of the time, Pallas kernels for 0%

commit v1 on v0

--- a/solution.py
+++ b/solution.py
@@ -2,8 +2,14 @@
 import jax.numpy as jnp
 from jax import lax
 from jax.sharding import PartitionSpec as P
+from jax.lax import all_to_all, axis_size
 
 TILE = 64
+
+
+def _arrange_strings(vector, named_axis, dim_k):
+    far_arr = jnp.stack([vector] * axis_size(named_axis))
+    return jnp.concatenate(all_to_all(far_arr, named_axis, 0, 0), axis=dim_k)
 
 
 def swap_in_tile(rows):
@@ -68,7 +74,7 @@
     running = running + jnp.where(keep > 1, second, jnp.zeros_like(second))
     third_int = jnp.where(take > 0, recv_int, jnp.where(take_y > 0, recv_int_y, integrals[2]))
     third_amp = jnp.where(take > 0, recv_amp, jnp.where(take_y > 0, recv_amp_y, own_amps(2)))
-    third = tile_product(third_amp, lax.all_gather(third_int, "pair", axis=0, tiled=True))
+    third = tile_product(third_amp, _arrange_strings(third_int, "pair", 0))
     third_live = (take > 0) | (take_y > 0) | (keep > 2)
     running = running + jnp.where(third_live, third, jnp.zeros_like(third))
 

time: 165 us -> 269 us (1.63)
  waiting for transfers between devices: 48.7 us -> 139 us
  starting transfers between devices: 15 us -> 25.7 us
  local copies, waits for them, and re-layouts: 36.9 us -> 40.3 us
    all_gather x1, waiting for transfers between devices: 0.01 us -> 110 us  [on_device(): first_two = lax.all_gather(integrals[0:2], 'pair', axis=1, tiled=True)]
    all_gather x1 -> x0, waiting for transfers between devices: 20.6 us -> none  [on_device(): lax.all_gather(third_int, 'pair', axis=0, tiled=True)]
    all_to_all x0 -> x1, starting transfers between devices: none -> 10.3 us  [_arrange_strings(): return jnp.concatenate(all_to_all(far_arr, named_axis, 0, 0), axis=dim_k)]
    another operation x0 -> x1, local copies, waits for them, and re-layouts: none -> 3.39 us  [_arrange_strings(): far_arr = jnp.stack([vector] * axis_size(named_axis))]
  transfers between devices with their start and end apart: 7 -> 7, of which waited for: 6 -> 6; matrix products, arithmetic and copies ran while one was open for 41% -> 26% of each run, Pallas kernels for 0% -> 0%
where the time goes in v1:
time: 269 us; the launch traced here: 268 us
  waiting for transfers between devices  139 us (52%)
  local copies, waits for them, and re-layouts  40.3 us (15%)
  matrix products  26.4 us (10%)
  starting transfers between devices  25.7 us (10%)
  between operations  21.9 us (8%)
  other arithmetic  14.2 us (5%)
    all_gather x1, waiting for transfers between devices, on_device(): first_two = lax.all_gather(integrals[0:2], 'pair', axis=1, tiled=True)  110 us
    dot_general x3, matrix products, tile_product(): lax.dot_general(amp_tile, int_rows, (((1,), (1,)), ((), ())), precision=p...  26.4 us
    ppermute x1, waiting for transfers between devices, on_device(): recv_amp = lax.ppermute(send_amp, 'virt', perm)  14.4 us
    unnamed x35, local copies, waits for them, and re-layouts  11.1 us
    all_to_all x1, starting transfers between devices, _arrange_strings(): return jnp.concatenate(all_to_all(far_arr, named_axis, 0, 0), axis=dim_k)  10.3 us
    mul x5, local copies, waits for them, and re-layouts, symmetric_amps(): return amp_rows + flag.astype(jnp.float32) * swap_in_tile(amp_rows)  10.1 us
    slice x2, local copies, waits for them, and re-layouts, own_amps(): return symmetric_amps(amplitudes[slot], tile_flags[slot])  9.12 us
    add x4, other arithmetic, symmetric_amps(): return amp_rows + flag.astype(jnp.float32) * swap_in_tile(amp_rows)  8.01 us
  transfers between devices with their start and end apart: 7, of which 6 were waited for; matrix products, arithmetic and copies ran while one was open for 26% of the time, Pallas kernels for 0%

profile of v1, /device:TPU:1, one launch (start us, length us, event | category | flops | bytes accessed | tf_op | source)
XLA Modules:
  0.0 267.9 jit_solution(8425604484905069004)
XLA Ops:
  7.2 2.2 slice.66
  11.4 3.6 %collective-permute-start.2 = (f32[24,4096]{1,0:T(8,128)S(1)}, f32[24,4096]{1,0:T(8,128)S(1)}, u32[]{:S(2)}, u32[]{:S(2)}) collective-permute-start(f32[24,4096]{1,0:T(8,128)S(1)} %get-tuple-element.42), channel_id=1, source_target_pairs={{0,8},{1,9},{2,10},{3,11},{4,12},{5,13},{6,14},{7,15},{8,0},{9,1},... | collective-permute-start | bytes 1179656 | tf_op jit(solution)/shard_map/ppermute | solution.py:62
  22.9 1.9 collective-permute-done.3
  24.8 3.4 %stack.2 = f32[16,24,4096]{2,1,0:T(8,128)} broadcast(f32[24,4096]{1,0:T(8,128)S(1)} %fusion.21), dimensions={1,2} | broadcast | bytes 6684672 | tf_op jit(solution)/shard_map/stack | solution.py:11
  28.2 10.3 %all-to-all-start = ((f32[16,24,4096]{2,1,0:T(8,128)}), f32[16,24,4096]{2,1,0:T(8,128)}, u32[]{:S(2)}, u32[]{:S(2)}) async-start(f32[16,24,4096]{2,1,0:T(8,128)} %stack.2), calls=%async_computation | async-start | bytes 12582912 | tf_op jit(solution)/shard_map/all_to_all | solution.py:12
  38.5 8.5 %fusion.25 = (f32[1,128,4096]{2,1,0:T(8,128)}, f32[1,128,4096]{2,1,0:T(8,128)}, f32[1,128,4096]{2,1,0:T(8,128)}, f32[1,128,4096]{2,1,0:T(8,128)}, f32[1,128,4096]{2,1,0:T(8,128)}) fusion(f32[4,128,4096]{2,1,0:T(8,128)} %param.9, s32[]{:T(128)S(6)} %select_n.101), kind=kLoop, calls=%fused_computation.59 | loop fusion | bytes 20971524 | tf_op jit(solution)/shard_map/slice | solution.py:69
  47.0 1.9 copy.41
  54.5 1.9 copy.42
  61.5 1.9 copy.43
  64.7 2.6 copy.37
  67.3 1.9 copy.40
  70.0 2.5 copy.31
  73.1 2.9 %copy.39 = f32[1,128,4096]{1,2,0:T(8,128)} copy(f32[1,128,4096]{2,1,0:T(8,128)} %get-tuple-element.40) | data formatting | bytes 4194304
  78.4 2.5 copy.29
  82.9 3.3 %bitcast_add_fusion.4 = f32[1,128,4096]{1,2,0:T(8,128)} fusion(f32[1,128,4096]{1,2,0:T(8,128)S(1)} %copy.40, f32[128,64,64]{0,2,1:T(8,128)} %copy.31), kind=kLoop, calls=%fused_computation.19 | loop fusion | flops 524288 | bytes 6291456 | tf_op jit(solution)/shard_map/add | solution.py:21
  87.7 14.4 %collective-permute-done = f32[128,4096]{0,1:T(8,128)} collective-permute-done((f32[128,4096]{0,1:T(8,128)}, f32[128,4096]{0,1:T(8,128)}, u32[]{:S(2)}, u32[]{:S(2)}) %collective-permute-start) | collective-permute-done | bytes 2097184 | tf_op jit(solution)/shard_map/ppermute | solution.py:63
  102.0 5.1 %collective-permute-done.1 = f32[128,4096]{0,1:T(8,128)} collective-permute-done((f32[128,4096]{0,1:T(8,128)}, f32[128,4096]{0,1:T(8,128)}, u32[]{:S(2)}, u32[]{:S(2)}) %collective-permute-start.1) | collective-permute-done | bytes 2097184 | tf_op jit(solution)/shard_map/ppermute | solution.py:66
  107.2 2.2 fusion.11
  109.4 109.9 %all-gather.6.cloned.1.call-done = f32[2,384,4096]{2,1,0:T(8,128)} async-done(((f32[2,24,4096]{2,1,0:T(8,128)}), f32[2,384,4096]{2,1,0:T(8,128)}) %all-gather.6.cloned.1.call-update) | async-done | bytes 12582928 | tf_op jit(solution)/shard_map/all_gather | solution.py:71
  219.2 9.5 %fusion.17 = f32[128,384]{1,0:T(8,128)S(1)} fusion(f32[2,384,4096]{2,1,0:T(8,128)} %all-gather.6.cloned.1.call-done, f32[1,128,4096]{1,2,0:T(8,128)S(1)} %copy-done.4, pred[]{:T(512)S(6)} %gt.29), kind=kOutput, calls=%fused_computation.23 | convolution fusion | flops 2415968256 | bytes 8585217 | tf_op jit(solution)/shard_map/dot_general | solution.py:25
  228.8 9.7 %fusion.14 = f32[128,384]{1,0:T(8,128)S(1)} fusion(f32[128,384]{1,0:T(8,128)S(1)} %fusion.17, f32[2,384,4096]{2,1,0:T(8,128)} %all-gather.6.cloned.1.call-done, f32[1,128,4096]{1,2,0:T(8,128)S(1)} %copy-done.5), kind=kOutput, calls=%fused_computation.22 | convolution fusion | flops 2415968256 | bytes 8781824 | tf_op jit(solution)/shard_map/dot_general | solution.py:25
  238.5 7.1 %fusion.20 = f32[128,384]{1,0:T(8,128)} fusion(f32[128,384]{1,0:T(8,128)S(1)} %fusion.14, f32[128,4096]{0,1:T(8,128)S(1)} %copy-done.6, f32[384,4096]{1,0:T(8,128)} %bitcast.42, pred[]{:T(512)S(6)} %or.7), kind=kOutput, calls=%fused_computation.25 | convolution fusion | flops 1208057856 | bytes 8781825 | tf_op jit(solution)/shard_map/dot_general | solution.py:25
  245.6 7.7 %all-to-all-start.1 = ((f32[16,8,384]{2,1,0:T(8,128)}), f32[16,8,384]{2,1,0:T(8,128)S(1)}, u32[]{:S(2)}, u32[]{:S(2)}) async-start(f32[16,8,384]{2,1,0:T(8,128)} %bitcast.43), calls=%async_computation.1 | async-start | bytes 393216 | tf_op jit(solution)/shard_map/all_to_all | solution.py:90
  253.6 6.8 %all-to-all-done.1 = f32[16,8,384]{2,1,0:T(8,128)S(1)} async-done(((f32[16,8,384]{2,1,0:T(8,128)}), f32[16,8,384]{2,1,0:T(8,128)S(1)}, u32[]{:S(2)}, u32[]{:S(2)}) %all-to-all-start.1) | async-done | bytes 196640 | tf_op jit(solution)/shard_map/all_to_all | solution.py:90
  (67 shorter events, 22.3 us)
Async XLA Ops:
  7.2 4.2 %copy-start.8 = (f32[4,24,4096]{2,1,0:T(8,128)S(1)}, f32[4,24,4096]{2,1,0:T(8,128)}, u32[]{:S(2)}) copy-start(f32[4,24,4096]{2,1,0:T(8,128)} %param.10) | copy-start | bytes 4718596
  7.2 2.3 copy-start.11
  7.2 212.0 %all-gather.6.cloned.1.call-start = ((), (), s32[]{:S(2)}) async-start(), calls=%async_computation.3 | async-start | bytes 13369344 | tf_op jit(solution)/shard_map/all_gather | solution.py:71
  11.4 11.4 %collective-permute-start.2 = (f32[24,4096]{1,0:T(8,128)S(1)}, f32[24,4096]{1,0:T(8,128)S(1)}, u32[]{:S(2)}, u32[]{:S(2)}) collective-permute-start(f32[24,4096]{1,0:T(8,128)S(1)} %get-tuple-element.42), channel_id=1, source_target_pairs={{0,8},{1,9},{2,10},{3,11},{4,12},{5,13},{6,14},{7,15},{8,0},{9,1},... | collective-permute-start | bytes 1179656 | tf_op jit(solution)/shard_map/ppermute | solution.py:62
  15.1 9.7 %collective-permute-start.3 = (f32[24,4096]{1,0:T(8,128)S(1)}, f32[24,4096]{1,0:T(8,128)S(1)}, u32[]{:S(2)}, u32[]{:S(2)}) collective-permute-start(f32[24,4096]{1,0:T(8,128)S(1)} %get-tuple-element.41), channel_id=1, source_target_pairs={{0,1},{1,0},{2,3},{3,2},{4,5},{5,4},{6,7},{7,6},{8,9},{9,8},{10,11... | collective-permute-start | bytes 1179656 | tf_op jit(solution)/shard_map/ppermute | solution.py:65
  28.2 210.3 %all-to-all-start = ((f32[16,24,4096]{2,1,0:T(8,128)}), f32[16,24,4096]{2,1,0:T(8,128)}, u32[]{:S(2)}, u32[]{:S(2)}) async-start(f32[16,24,4096]{2,1,0:T(8,128)} %stack.2), calls=%async_computation | async-start | bytes 12582912 | tf_op jit(solution)/shard_map/all_to_all | solution.py:12
  47.0 1.9 copy-start.10
  53.1 48.9 %collective-permute-start = (f32[128,4096]{0,1:T(8,128)}, f32[128,4096]{0,1:T(8,128)}, u32[]{:S(2)}, u32[]{:S(2)}) collective-permute-start(f32[128,4096]{0,1:T(8,128)} %bitcast_add_fusion.3), channel_id=1, source_target_pairs={{0,8},{1,9},{2,10},{3,11},{4,12},{5,13},{6,14},{7,15},{8,0},{9,1},... | collective-permute-start | bytes 6291464 | tf_op jit(solution)/shard_map/ppermute | solution.py:63
  60.1 47.0 %collective-permute-start.1 = (f32[128,4096]{0,1:T(8,128)}, f32[128,4096]{0,1:T(8,128)}, u32[]{:S(2)}, u32[]{:S(2)}) collective-permute-start(f32[128,4096]{0,1:T(8,128)} %bitcast_add_fusion.2), channel_id=1, source_target_pairs={{0,1},{1,0},{2,3},{3,2},{4,5},{5,4},{6,7},{7,6},{8,9},{9,8},{10,11... | collective-permute-start | bytes 6291464 | tf_op jit(solution)/shard_map/ppermute | solution.py:66
  63.4 1.3 copy-start.1
  82.9 3.3 %copy-start = (f32[1,128,4096]{1,2,0:T(8,128)S(1)}, f32[1,128,4096]{1,2,0:T(8,128)}, u32[]{:S(2)}) copy-start(f32[1,128,4096]{1,2,0:T(8,128)} %copy.39) | copy-start | bytes 6291460
  82.9 3.3 %copy-start.3 = (f32[128,64,64]{0,2,1:T(8,128)S(1)}, f32[128,64,64]{0,2,1:T(8,128)}, u32[]{:S(2)}) copy-start(f32[128,64,64]{0,2,1:T(8,128)} %copy.29) | copy-start | bytes 6291460
  86.2 21.0 %copy-start.2 = (f32[1,128,4096]{1,2,0:T(8,128)S(1)}, f32[1,128,4096]{1,2,0:T(8,128)}, u32[]{:S(2)}) copy-start(f32[1,128,4096]{1,2,0:T(8,128)} %copy-done.1) | copy-start | bytes 6291460
  86.2 21.0 %copy-start.7 = (f32[128,64,64]{0,2,1:T(8,128)S(1)}, f32[128,64,64]{0,2,1:T(8,128)}, u32[]{:S(2)}) copy-start(f32[128,64,64]{0,2,1:T(8,128)} %copy.37) | copy-start | bytes 6291460
  87.7 131.6 %copy-start.4 = (f32[1,128,4096]{1,2,0:T(8,128)S(1)}, f32[1,128,4096]{1,2,0:T(8,128)}, u32[]{:S(2)}) copy-start(f32[1,128,4096]{1,2,0:T(8,128)} %bitcast_add_fusion.4) | copy-start | bytes 6291460
  219.2 9.5 %copy-start.5 = (f32[1,128,4096]{1,2,0:T(8,128)S(1)}, f32[1,128,4096]{1,2,0:T(8,128)}, u32[]{:S(2)}) copy-start(f32[1,128,4096]{1,2,0:T(8,128)} %bitcast_add_fusion.5) | copy-start | bytes 6291460
  228.8 9.8 %copy-start.6 = (f32[128,4096]{0,1:T(8,128)S(1)}, f32[128,4096]{0,1:T(8,128)}, u32[]{:S(2)}) copy-start(f32[128,4096]{0,1:T(8,128)} %fusion.11) | copy-start | bytes 6291460
  245.6 7.7 %copy-start.14 = (s32[8,2]{0,1:T(2,128)S(1)}, s32[8,2]{0,1:T(2,128)}, u32[]{:S(2)}) copy-start(s32[8,2]{0,1:T(2,128)} %param.13) | copy-start | bytes 196
  245.6 7.7 %copy-start.13 = (f32[200]{0:T(256)S(1)}, f32[200]{0:T(256)}, u32[]{:S(2)}) copy-start(f32[200]{0:T(256)} %param.14) | copy-start | bytes 2404
  245.6 14.7 %copy-start.12 = (f32[384]{0:T(512)S(1)}, f32[384]{0:T(512)}, u32[]{:S(2)}) copy-start(f32[384]{0:T(512)} %param.15) | copy-start | bytes 4612
  245.6 14.7 %all-to-all-start.1 = ((f32[16,8,384]{2,1,0:T(8,128)}), f32[16,8,384]{2,1,0:T(8,128)S(1)}, u32[]{:S(2)}, u32[]{:S(2)}) async-start(f32[16,8,384]{2,1,0:T(8,128)} %bitcast.43), calls=%async_computation.1 | async-start | bytes 393216 | tf_op jit(solution)/shard_map/all_to_all | solution.py:90
  260.4 0.7 copy-start.9
Sparse Core Ops, SparseCore 0:
  9.8 209.3 all-gather.5
